TPU v7x, 32 devices: a whole 2x2x4 slice. The times are simulated.
32 devices in a mesh: tile: 8 (over y, x, core), mem: 4 (over z).
Axes of the slice: x: 2, y: 2, z: 4, core: 2. Of those that a mesh axis runs over, the one named last changes fastest.
Arguments:
- control: bfloat16 [80, 1, 360, 720], P('mem', None, 'tile'), may hold values from -6 to 6
- perturb: bfloat16 [80, 1, 360, 720], P('mem', None, 'tile'), may hold values from -6 to 6
- lon_taps: bfloat16 [17], replicated, may hold values from 0.026367188 to 0.07910156
- lat_taps: bfloat16 [17], replicated, may hold values from 0.026367188 to 0.07910156
- innov: float32 [8, 8, 256], P('tile'), may hold values from -6 to 6
- inv_var: float32 [8, 8, 256], P('tile'), may hold values from 1 to 8
- cell_index: int32 [8, 8, 256], P('tile'), may hold values from 0 to 32399, as said below
- counts: int32 [8, 8], P('tile'), may hold values from 0 to 256, as said below
Outputs:
- gradient: float32 [80, 1, 360, 720], P('mem', None, 'tile')
Inputs may be any that keep to these rules, and one draw needn't show every extreme that they name: `cell_index`: an observation's cell within its owning tile, level * 45 * 720 + longitude within the tile * 720 + latitude; both ends are taken. `counts`: live slots per pair of tiles; some pair fills all 256 slots in every draw, and some owning tiles receive far more than others.
All inputs are finite; a program needn't handle non-finite values.
Results may differ from a plain program's by a relative error of at most 0.00066.
Values may be sent and summed in bfloat16 or wider, within the bound.
No kernel may reach another device: no remote copies, remote signals or barrier semaphores. Data moves between devices by JAX's collectives and lax.ppermute only.
A program may use at most 64 MiB of HBM per device.

v0:
```python
import math
import jax
import jax.numpy as jnp
from jax import lax
from jax.sharding import PartitionSpec as P


def extended_2(block, sides, width):
    for axis, dim in sides:
        count = lax.axis_size(axis)
        forward = [(i, i + 1) for i in range(count - 1)]
        forward.append((count - 1, 0))
        backward = [(target, source) for source, target in forward]
        low = lax.ppermute(
            lax.slice_in_dim(block, block.shape[dim] - width, None, axis=dim), axis, forward
        )
        high = lax.ppermute(lax.slice_in_dim(block, 0, width, axis=dim), axis, backward)
        block = jnp.concatenate([low, block, high], axis=dim)
    return block


def band_from(offsets, tap_weights):
    radius = tap_weights.shape[0] - 1
    taps = tap_weights.astype(jnp.float32)
    band = jnp.zeros(offsets.shape, jnp.float32)
    for offset in range(radius + 1):
        band = band + jnp.where(offsets == offset, taps[offset], 0.0)
    return band.astype(jnp.bfloat16)


def lon_band(tap_weights, lon_cells):
    radius = tap_weights.shape[0] - 1
    row_ids = lax.broadcasted_iota(jnp.int32, (lon_cells, lon_cells + 2 * radius), 0)
    col_ids = lax.broadcasted_iota(jnp.int32, (lon_cells, lon_cells + 2 * radius), 1)
    return band_from(jnp.abs(col_ids - row_ids - radius), tap_weights)


def lat_block_band(tap_weights, block_cells):
    radius = tap_weights.shape[0] - 1
    row_ids = lax.broadcasted_iota(jnp.int32, (block_cells + 2 * radius, block_cells), 0)
    col_ids = lax.broadcasted_iota(jnp.int32, (block_cells + 2 * radius, block_cells), 1)
    return band_from(jnp.abs(row_ids - radius - col_ids), tap_weights)


def localize(extended, band_lon, band_blocks, radius, block_cells):
    along = jnp.einsum(
        "ij,mljk->mlik", band_lon, extended, preferred_element_type=jnp.float32
    ).astype(jnp.bfloat16)
    members_here, levels, lon_cells, lat_cells = along.shape
    padded = jnp.pad(along, ((0, 0), (0, 0), (0, 0), (radius, radius)))
    block_count = lat_cells // block_cells
    windows = jnp.stack(
        [
            padded[:, :, :, block * block_cells : block * block_cells + block_cells + 2 * radius]
            for block in range(block_count)
        ],
        axis=3,
    )
    result = jnp.einsum("mlibk,kq->mlibq", windows, band_blocks, preferred_element_type=jnp.float32)
    return result.reshape(members_here, levels, lon_cells, lat_cells)


def pick_cells(field_rows, row_index, col_index, block_rows):
    row_count, col_count = field_rows.shape
    field_cols = field_rows.T

    def pick_one_block(indices):
        rows_here, cols_here = indices
        onehot_rows = (
            rows_here[:, None] == jnp.arange(row_count, dtype=jnp.int32)[None, :]
        ).astype(jnp.float32)
        onehot_cols = (
            cols_here[:, None] == jnp.arange(col_count, dtype=jnp.int32)[None, :]
        ).astype(jnp.float32)
        picked = jnp.dot(
            onehot_cols,
            field_cols,
            precision=lax.Precision.HIGHEST,
            preferred_element_type=jnp.float32,
        )
        return jnp.sum(picked * onehot_rows, axis=1)

    values = lax.map(
        pick_one_block, (row_index.reshape(-1, block_rows), col_index.reshape(-1, block_rows))
    )
    return values.reshape(-1)


def spread_cells(misfit, row_index, col_index, row_count, col_count, block_rows):

    def spread_one_block(total, items):
        rows_here, cols_here, values = items
        onehot_rows = (
            rows_here[:, None] == jnp.arange(row_count, dtype=jnp.int32)[None, :]
        ).astype(jnp.float32)
        onehot_cols = (
            cols_here[:, None] == jnp.arange(col_count, dtype=jnp.int32)[None, :]
        ).astype(jnp.float32)
        weighted = onehot_rows * values[:, None]
        return (
            total
            + jnp.dot(
                weighted.T,
                onehot_cols,
                precision=lax.Precision.HIGHEST,
                preferred_element_type=jnp.float32,
            ),
            None,
        )

    start = jnp.zeros((row_count, col_count), jnp.float32)
    items = (
        row_index.reshape(-1, block_rows),
        col_index.reshape(-1, block_rows),
        misfit.reshape(-1, block_rows),
    )
    total, _ = lax.scan(spread_one_block, start, items)
    return total


def local(control, perturb, lon_taps, lat_taps, innov, inv_var, cell_index, counts):
    members_here, levels, lon_cells, lat_cells = control.shape
    radius = lon_taps.shape[0] - 1
    block_cells = 144
    band_lon = lon_band(lon_taps, lon_cells)
    band_blocks = lat_block_band(lat_taps, block_cells)
    extended = extended_2(control, (("tile", 2),), radius)
    smoothed = localize(extended, band_lon, band_blocks, radius, block_cells)
    member_sum = jnp.sum(perturb.astype(jnp.float32) * smoothed, axis=0)
    slot_ids = lax.broadcasted_iota(jnp.int32, innov.shape, 2)
    is_live = slot_ids < counts[:, :, None]
    weights = jnp.where(is_live, inv_var, 0.0)
    received = (
        lax.all_to_all(innov, "tile", split_axis=1, concat_axis=0, tiled=True),
        lax.all_to_all(weights, "tile", split_axis=1, concat_axis=0, tiled=True),
        lax.all_to_all(cell_index, "tile", split_axis=1, concat_axis=0, tiled=True),
    )
    observed = received[0].reshape(-1)
    weight_recv = received[1].reshape(-1)
    cells_hit = received[2].reshape(-1)
    row_index = cells_hit // lat_cells
    col_index = cells_hit % lat_cells
    row_count = levels * lon_cells
    block_rows = math.gcd(observed.shape[0], 1024)
    increment = lax.psum(member_sum, "mem")
    at_cells = pick_cells(increment.reshape(row_count, lat_cells), row_index, col_index, block_rows)
    misfit = weight_recv * (at_cells - observed)
    spread = spread_cells(misfit, row_index, col_index, row_count, lat_cells, block_rows)
    spread = spread.reshape(levels, lon_cells, lat_cells)
    wide_pert = extended_2(perturb, (("tile", 2),), radius)
    wide_spread = extended_2(spread, (("tile", 1),), radius)
    wide_products = (wide_pert.astype(jnp.float32) * wide_spread[None]).astype(jnp.bfloat16)
    return control.astype(jnp.float32) + localize(
        wide_products, band_lon, band_blocks, radius, block_cells
    )


def solution(mesh):
    return jax.shard_map(
        local,
        mesh=mesh,
        in_specs=(
            P("mem", None, "tile", None),
            P("mem", None, "tile", None),
            P(),
            P(),
            P("tile", None, None),
            P("tile", None, None),
            P("tile", None, None),
            P("tile", None),
        ),
        out_specs=P("mem", None, "tile", None),
        check_vma=False,
    )
```

profile of v0, /device:TPU:11, one launch (start us, length us, event | category | flops | bytes accessed | tf_op | source)
XLA Modules:
  0.0 176.9 jit_solution(8008073635435257452)
XLA Ops:
  6.6 1.5 fusion.166
  8.1 1.8 %collective-permute-start.2 = (bf16[20,1,16,720]{3,2,0,1:T(8,128)(2,1)S(1)}, bf16[20,1,16,720]{3,2,0,1:T(8,128)(2,1)}, u32[]{:S(2)}, u32[]{:S(2)}) collective-permute-start(bf16[20,1,16,720]{3,2,0,1:T(8,128)(2,1)S(1)} %get-tuple-element.115), channel_id=1, source_target_pairs={{0,4},{4,8},{8,12},{12,16},{16,20},{20,24},{24,28},{28,0},{1,5},{5... | collective-permute-start | bytes 1382408 | tf_op jit(solution)/shard_map/ppermute | solution.py:14
  9.9 1.3 copy.48
  11.2 4.9 %all-to-all-start = ((s32[1,8,256]{2,0,1:T(1,128)}), s32[1,8,256]{2,0,1:T(1,128)S(1)}, u32[]{:S(2)}, u32[]{:S(2)}) async-start(s32[1,8,256]{2,0,1:T(1,128)} %copy.48), calls=%async_computation | async-start | bytes 16384 | tf_op jit(solution)/shard_map/all_to_all | solution.py:136
  16.1 2.2 %fusion.167 = (bf16[20,1,16,720]{3,2,0,1:T(8,128)(2,1)}, bf16[20,1,16,720]{3,2,0,1:T(8,128)(2,1)S(1)}) fusion(bf16[20,1,45,720]{3,2,0,1:T(8,128)(2,1)} %bitcast.147), kind=kLoop, calls=%fused_computation.200 | loop fusion | bytes 1843200 | tf_op jit(solution)/shard_map/slice | solution.py:15
  18.3 1.5 collective-permute-start
  19.8 0.7 compare_select_fusion
  20.4 0.7 fusion.170
  21.2 0.7 fusion.169
  21.9 0.6 copy.57
  22.5 0.7 all-to-all-done
  23.2 4.4 %all-to-all-start.1 = ((f32[1,8,256]{2,0,1:T(1,128)}), f32[1,8,256]{2,0,1:T(1,128)S(1)}, u32[]{:S(2)}, u32[]{:S(2)}) async-start(f32[1,8,256]{2,0,1:T(1,128)} %compare_select_fusion), calls=%async_computation.1 | async-start | bytes 16384 | tf_op jit(solution)/shard_map/all_to_all | solution.py:135
  27.6 0.1 remainder_reduce_fusion
  27.7 5.6 %all-to-all-done.1 = f32[1,8,256]{2,0,1:T(1,128)S(1)} async-done(((f32[1,8,256]{2,0,1:T(1,128)}), f32[1,8,256]{2,0,1:T(1,128)S(1)}, u32[]{:S(2)}, u32[]{:S(2)}) %all-to-all-start.1) | async-done | bytes 8224 | tf_op jit(solution)/shard_map/all_to_all | solution.py:135
  33.4 4.0 %all-to-all-start.2 = ((f32[1,8,256]{2,0,1:T(1,128)}), f32[1,8,256]{2,0,1:T(1,128)S(1)}, u32[]{:S(2)}, u32[]{:S(2)}) async-start(f32[1,8,256]{2,0,1:T(1,128)} %copy.57), calls=%async_computation.2 | async-start | bytes 16384 | tf_op jit(solution)/shard_map/all_to_all | solution.py:134
  37.5 3.1 %all-to-all-done.2 = f32[1,8,256]{2,0,1:T(1,128)S(1)} async-done(((f32[1,8,256]{2,0,1:T(1,128)}), f32[1,8,256]{2,0,1:T(1,128)S(1)}, u32[]{:S(2)}, u32[]{:S(2)}) %all-to-all-start.2) | async-done | bytes 8224 | tf_op jit(solution)/shard_map/all_to_all | solution.py:134
  40.7 12.1 %fusion.31 = bf16[20,1,45,720]{3,2,0,1:T(8,128)(2,1)S(1)} fusion(bf16[20,1,16,720]{3,2,0,1:T(8,128)(2,1)} %collective-permute-done.3, bf16[20,1,45,720]{3,2,0,1:T(8,128)(2,1)S(1)} %bitcast.146, bf16[20,1,16,720]{3,2,0,1:T(8,128)(2,1)} %collective-permute-done.2, f32[]{:T(128)} %bitcast.31, f32[]{:T(128)} %bitcast.30, f32[]{:T(128)} %bitcast.29, ...), kind=kOutput, calls=%fused_computation.44 | convolution fusion | flops 107279912 | bytes 3513668 | tf_op jit(solution)/shard_map/ij,mljk->mlik/dot_general | solution.py:46
  52.7 0.2 fusion.33
  53.0 0.2 fusion.44
  53.2 0.2 fusion.43
  53.4 0.2 fusion.35
  53.7 11.5 %fusion.25 = f32[20,45,5,144]{3,1,2,0:T(8,128)S(1)} fusion(f32[]{:T(128)} %bitcast.58, f32[]{:T(128)} %bitcast.57, f32[]{:T(128)} %bitcast.56, f32[]{:T(128)} %bitcast.55, f32[]{:T(128)} %bitcast.54, f32[]{:T(128)} %bitcast.53, f32[]{:T(128)} %bitcast.52, f32[]{:T(128)} %bitcast.51, f32[]{:T(128)} %bitcast.50, f32[]{:T(128)} %bitcast.49, f32[]{:T(128)} %bitcast.48, ...), kind=kOutput, calls=%fused_computation.38 | convolution fusion | flops 229439232 | bytes 4176772 | tf_op jit(solution)/shard_map/mlibk,kq->mlibq/dot_general | solution.py:59
  65.2 6.4 %copy.55 = f32[20,45,5,144]{3,2,1,0:T(8,128)} copy(f32[20,45,5,144]{3,1,2,0:T(8,128)S(1)} %fusion.25) | data formatting | bytes 5184000 | tf_op jit(solution)/shard_map/mlibk,kq->mlibq/dot_general | solution.py:59
  71.6 4.9 %reshape.136 = f32[20,1,45,720]{3,2,0,1:T(8,128)S(1)} reshape(f32[20,45,5,144]{3,2,1,0:T(8,128)} %copy.55) | data formatting | bytes 5184000 | tf_op jit(solution)/shard_map/reshape | solution.py:60
  76.4 2.4 %multiply_reduce_fusion = f32[45,720]{1,0:T(8,128)} fusion(f32[20,1,45,720]{3,2,0,1:T(8,128)S(1)} %reshape.136, bf16[20,1,45,720]{3,2,1,0:T(8,128)(2,1)} %param.13), kind=kLoop, calls=%fused_computation.22 | loop fusion | flops 1911600 | bytes 4017600 | tf_op jit(solution)/shard_map/reduce_sum | solution.py:129
  78.9 32.7 %all-reduce.4.cloned.1.call-done = f32[720,45]{0,1:T(8,128)} async-done(((f32[720,45]{0,1:T(8,128)}), f32[720,45]{0,1:T(8,128)}) %all-reduce.4.cloned.1.call-update) | async-done | bytes 129616 | tf_op jit(solution)/shard_map/psum | solution.py:145
  111.6 1.1 copy.56
  112.7 3.8 %while.21 = (s32[]{:T(128)}, f32[2,1024]{1,0:T(2,128)S(1)}, s32[2,1024]{1,0:T(2,128)S(1)}, s32[2,1024]{1,0:T(2,128)S(1)}, f32[720,45]{1,0:T(8,128)S(1)}, /*index=5*/s32[]{:T(128)}, s32[]{:T(128)}) while((s32[]{:T(128)}, f32[2,1024]{1,0:T(2,128)S(1)}, s32[2,1024]{1,0:T(2,128)S(1)}, s32[2,1024]{1,0:T(2,128)S(1)}, f32[720,45]{1,0:T(8,128)S(1)}, ...), condition=%wide.region_4.5_spmd, body=%wide.region_2.4_spmd.sunk | while | flops 399005696 | bytes 166549 | solution.py:83
  112.7 1.8 %fusion.179 = f32[1024]{0:T(1024)S(1)} fusion(f32[720,45]{1,0:T(8,128)S(1)} %get-tuple-element.245, s32[1024]{0:T(1024)S(1)} %bitcast.156, s32[1024]{0:T(1024)S(1)} %bitcast.157), kind=kOutput, calls=%fused_computation.4.clone.1 | convolution fusion | flops 399005696 | bytes 141888 | tf_op jit(solution)/shard_map/while/body/eval_jaxpr/dot_general | solution.py:75
  114.5 0.1 dynamic_update_slice.5
  114.6 1.8 %fusion.179 = f32[1024]{0:T(1024)S(1)} fusion(f32[720,45]{1,0:T(8,128)S(1)} %get-tuple-element.245, s32[1024]{0:T(1024)S(1)} %bitcast.156, s32[1024]{0:T(1024)S(1)} %bitcast.157), kind=kOutput, calls=%fused_computation.4.clone.1 | convolution fusion | flops 399005696 | bytes 141888 | tf_op jit(solution)/shard_map/while/body/eval_jaxpr/dot_general | solution.py:75
  116.4 0.1 dynamic_update_slice.5
  116.5 3.1 %while.22 = (s32[]{:T(128)}, f32[45,720]{1,0:T(8,128)S(1)}, s32[2,1024]{1,0:T(2,128)S(1)}, f32[2,1024]{1,0:T(2,128)S(1)}, s32[2,1024]{1,0:T(2,128)S(1)}, /*index=5*/s32[]{:T(128)}, s32[]{:T(128)}) while((s32[]{:T(128)}, f32[45,720]{1,0:T(8,128)S(1)}, s32[2,1024]{1,0:T(2,128)S(1)}, f32[2,1024]{1,0:T(2,128)S(1)}, ...), condition=%wide.region_6.7_spmd.clone, body=%wide.region_5.6_spmd.clone.sunk | while | flops 399025440 | bytes 296159 | solution.py:117
  116.6 1.5 fusion.181
  118.1 1.5 fusion.181
  119.7 3.9 %collective-permute-start.4 = (f32[1,16,720]{2,1,0:T(8,128)S(1)}, f32[1,16,720]{2,1,0:T(8,128)S(1)}, u32[]{:S(2)}, u32[]{:S(2)}) collective-permute-start(f32[1,16,720]{2,1,0:T(8,128)S(1)} %get-tuple-element.119), channel_id=1, source_target_pairs={{0,4},{4,8},{8,12},{12,16},{16,20},{20,24},{24,28},{28,0},{1,5},{5... | collective-permute-start | bytes 138248 | tf_op jit(solution)/shard_map/ppermute | solution.py:14
  123.6 1.2 collective-permute-done.4
  124.7 3.2 %collective-permute-done.5 = f32[1,16,720]{2,1,0:T(8,128)S(1)} collective-permute-done((f32[1,16,720]{2,1,0:T(8,128)S(1)}, f32[1,16,720]{2,1,0:T(8,128)S(1)}, u32[]{:S(2)}, u32[]{:S(2)}) %collective-permute-start.5) | collective-permute-done | bytes 46112 | tf_op jit(solution)/shard_map/ppermute | solution.py:17
  128.0 12.3 %fusion.30 = bf16[20,1,45,720]{3,2,0,1:T(8,128)(2,1)S(1)} fusion(bf16[20,16,720]{2,1,0:T(8,128)(2,1)} %bitcast.8, bf16[20,45,720]{2,1,0:T(8,128)(2,1)S(1)} %bitcast.148, bf16[20,16,720]{2,1,0:T(8,128)(2,1)} %bitcast.5, f32[77,720]{1,0:T(8,128)S(1)} %maximum_bitcast_fusion.6, f32[]{:T(128)} %bitcast.31, f32[]{:T(128)} %bitcast.30, f32[]{:T(128)} %bitcast.29, ...), kind=kOutput, calls=%fused_computation.43 | convolution fusion | flops 109497512 | bytes 3735428 | tf_op jit(solution)/shard_map/ij,mljk->mlik/dot_general | solution.py:46
  140.3 0.2 fusion.37
  140.6 0.2 fusion.41
  140.8 0.2 fusion.40
  141.0 0.2 fusion.39
  141.2 11.5 %fusion.23 = f32[20,45,5,144]{3,1,2,0:T(8,128)S(1)} fusion(f32[]{:T(128)} %bitcast.58, f32[]{:T(128)} %bitcast.57, f32[]{:T(128)} %bitcast.56, f32[]{:T(128)} %bitcast.55, f32[]{:T(128)} %bitcast.54, f32[]{:T(128)} %bitcast.53, f32[]{:T(128)} %bitcast.52, f32[]{:T(128)} %bitcast.51, f32[]{:T(128)} %bitcast.50, f32[]{:T(128)} %bitcast.49, f32[]{:T(128)} %bitcast.48, ...), kind=kOutput, calls=%fused_computation.36 | convolution fusion | flops 229439232 | bytes 4176772 | tf_op jit(solution)/shard_map/mlibk,kq->mlibq/dot_general | solution.py:59
  152.7 6.4 %copy.59 = f32[20,45,5,144]{3,2,1,0:T(8,128)} copy(f32[20,45,5,144]{3,1,2,0:T(8,128)S(1)} %fusion.23) | data formatting | bytes 5184000 | tf_op jit(solution)/shard_map/mlibk,kq->mlibq/dot_general | solution.py:59
  159.1 4.9 %reshape.141 = f32[20,1,45,720]{3,2,0,1:T(8,128)S(1)} reshape(f32[20,45,5,144]{3,2,1,0:T(8,128)} %copy.59) | data formatting | bytes 5184000 | tf_op jit(solution)/shard_map/reshape | solution.py:60
  164.0 1.7 convert_add_fusion
  165.7 4.4 %copy.60 = f32[20,1,45,720]{3,1,2,0:T(1,128)} copy(f32[20,1,45,720]{3,2,0,1:T(8,128)S(1)} %convert_add_fusion) | data formatting | bytes 5184000 | tf_op jit(solution)/shard_map/add | solution.py:153
  (48 shorter events, 0.4 us)
Async XLA Ops:
  6.5 34.1 %copy-start = (bf16[20,1,45,720]{3,2,1,0:T(8,128)(2,1)S(1)}, bf16[20,1,45,720]{3,2,1,0:T(8,128)(2,1)}, u32[]{:S(2)}) copy-start(bf16[20,1,45,720]{3,2,1,0:T(8,128)(2,1)} %param.12) | copy-start | bytes 3888004
  6.5 13.2 %copy-start.7 = (s32[1,8]{1,0:T(1,128)S(1)}, s32[1,8]{1,0:T(1,128)}, u32[]{:S(2)}) copy-start(s32[1,8]{1,0:T(1,128)} %param.19) | copy-start | bytes 100
  6.5 13.2 %copy-start.5 = (f32[1,8,256]{2,1,0:T(8,128)S(1)}, f32[1,8,256]{2,1,0:T(8,128)}, u32[]{:S(2)}) copy-start(f32[1,8,256]{2,1,0:T(8,128)} %param.17) | copy-start | bytes 24580
  6.5 13.9 %copy-start.3 = (bf16[17]{0:T(256)(128)(2,1)S(1)}, bf16[17]{0:T(256)(128)(2,1)}, u32[]{:S(2)}) copy-start(bf16[17]{0:T(256)(128)(2,1)} %param.14) | copy-start | bytes 106
  6.5 14.6 %copy-start.4 = (bf16[17]{0:T(256)(128)(2,1)S(1)}, bf16[17]{0:T(256)(128)(2,1)}, u32[]{:S(2)}) copy-start(bf16[17]{0:T(256)(128)(2,1)} %param.15) | copy-start | bytes 106
  6.5 15.3 %copy-start.6 = (f32[1,8,256]{2,1,0:T(8,128)S(1)}, f32[1,8,256]{2,1,0:T(8,128)}, u32[]{:S(2)}) copy-start(f32[1,8,256]{2,1,0:T(8,128)} %param.16) | copy-start | bytes 24580
  8.1 32.6 %collective-permute-start.2 = (bf16[20,1,16,720]{3,2,0,1:T(8,128)(2,1)S(1)}, bf16[20,1,16,720]{3,2,0,1:T(8,128)(2,1)}, u32[]{:S(2)}, u32[]{:S(2)}) collective-permute-start(bf16[20,1,16,720]{3,2,0,1:T(8,128)(2,1)S(1)} %get-tuple-element.115), channel_id=1, source_target_pairs={{0,4},{4,8},{8,12},{12,16},{16,20},{20,24},{24,28},{28,0},{1,5},{5... | collective-permute-start | bytes 1382408 | tf_op jit(solution)/shard_map/ppermute | solution.py:14
  9.9 30.7 %collective-permute-start.3 = (bf16[20,1,16,720]{3,2,0,1:T(8,128)(2,1)S(1)}, bf16[20,1,16,720]{3,2,0,1:T(8,128)(2,1)}, u32[]{:S(2)}, u32[]{:S(2)}) collective-permute-start(bf16[20,1,16,720]{3,2,0,1:T(8,128)(2,1)S(1)} %get-tuple-element.116), channel_id=1, source_target_pairs={{4,0},{8,4},{12,8},{16,12},{20,16},{24,20},{28,24},{0,28},{5,1},{9... | collective-permute-start | bytes 1382408 | tf_op jit(solution)/shard_map/ppermute | solution.py:17
  11.2 12.0 %all-to-all-start = ((s32[1,8,256]{2,0,1:T(1,128)}), s32[1,8,256]{2,0,1:T(1,128)S(1)}, u32[]{:S(2)}, u32[]{:S(2)}) async-start(s32[1,8,256]{2,0,1:T(1,128)} %copy.48), calls=%async_computation | async-start | bytes 16384 | tf_op jit(solution)/shard_map/all_to_all | solution.py:136
  18.3 109.7 %collective-permute-start = (bf16[20,1,16,720]{3,2,0,1:T(8,128)(2,1)}, bf16[20,1,16,720]{3,2,0,1:T(8,128)(2,1)}, u32[]{:S(2)}, u32[]{:S(2)}) collective-permute-start(bf16[20,1,16,720]{3,2,0,1:T(8,128)(2,1)} %get-tuple-element.117), channel_id=1, source_target_pairs={{0,4},{4,8},{8,12},{12,16},{16,20},{20,24},{24,28},{28,0},{1,5},{5... | collective-permute-start | bytes 1382408 | tf_op jit(solution)/shard_map/ppermute | solution.py:14
  19.8 108.2 %collective-permute-start.1 = (bf16[20,1,16,720]{3,2,0,1:T(8,128)(2,1)S(1)}, bf16[20,1,16,720]{3,2,0,1:T(8,128)(2,1)}, u32[]{:S(2)}, u32[]{:S(2)}) collective-permute-start(bf16[20,1,16,720]{3,2,0,1:T(8,128)(2,1)S(1)} %get-tuple-element.118), channel_id=1, source_target_pairs={{4,0},{8,4},{12,8},{16,12},{20,16},{24,20},{28,24},{0,28},{5,1},{9... | collective-permute-start | bytes 1382408 | tf_op jit(solution)/shard_map/ppermute | solution.py:17
  23.2 10.1 %all-to-all-start.1 = ((f32[1,8,256]{2,0,1:T(1,128)}), f32[1,8,256]{2,0,1:T(1,128)S(1)}, u32[]{:S(2)}, u32[]{:S(2)}) async-start(f32[1,8,256]{2,0,1:T(1,128)} %compare_select_fusion), calls=%async_computation.1 | async-start | bytes 16384 | tf_op jit(solution)/shard_map/all_to_all | solution.py:135
  33.4 7.2 %all-to-all-start.2 = ((f32[1,8,256]{2,0,1:T(1,128)}), f32[1,8,256]{2,0,1:T(1,128)S(1)}, u32[]{:S(2)}, u32[]{:S(2)}) async-start(f32[1,8,256]{2,0,1:T(1,128)} %copy.57), calls=%async_computation.2 | async-start | bytes 16384 | tf_op jit(solution)/shard_map/all_to_all | solution.py:134
  37.3 74.3 %all-reduce.4.cloned.1.call-start = ((), (), s32[]{:S(2)}) async-start(), calls=%async_computation.3 | async-start | bytes 294912 | tf_op jit(solution)/shard_map/psum | solution.py:145
  112.7 3.8 %copy-start.2 = (f32[45,720]{1,0:T(8,128)S(1)}, f32[45,720]{1,0:T(8,128)}, u32[]{:S(2)}) copy-start(f32[45,720]{1,0:T(8,128)} %custom-call) | copy-start | bytes 388804
  116.5 11.5 %copy-start.1 = (bf16[20,1,45,720]{3,2,1,0:T(8,128)(2,1)S(1)}, bf16[20,1,45,720]{3,2,1,0:T(8,128)(2,1)}, u32[]{:S(2)}) copy-start(bf16[20,1,45,720]{3,2,1,0:T(8,128)(2,1)} %param.13) | copy-start | bytes 3888004
  119.7 5.1 %collective-permute-start.4 = (f32[1,16,720]{2,1,0:T(8,128)S(1)}, f32[1,16,720]{2,1,0:T(8,128)S(1)}, u32[]{:S(2)}, u32[]{:S(2)}) collective-permute-start(f32[1,16,720]{2,1,0:T(8,128)S(1)} %get-tuple-element.119), channel_id=1, source_target_pairs={{0,4},{4,8},{8,12},{12,16},{16,20},{20,24},{24,28},{28,0},{1,5},{5... | collective-permute-start | bytes 138248 | tf_op jit(solution)/shard_map/ppermute | solution.py:14
  123.5 4.4 %collective-permute-start.5 = (f32[1,16,720]{2,1,0:T(8,128)S(1)}, f32[1,16,720]{2,1,0:T(8,128)S(1)}, u32[]{:S(2)}, u32[]{:S(2)}) collective-permute-start(f32[1,16,720]{2,1,0:T(8,128)S(1)} %get-tuple-element.120), channel_id=1, source_target_pairs={{4,0},{8,4},{12,8},{16,12},{20,16},{24,20},{28,24},{0,28},{5,1},{9... | collective-permute-start | bytes 138248 | tf_op jit(solution)/shard_map/ppermute | solution.py:17
Sparse Core Ops, SparseCore 0:
  79.0 32.5 all-reduce.3
where the time goes:
time: 178 us; the launch traced here: 177 us
  matrix products  54 us (30%)
  waiting for transfers between devices  46.7 us (26%)
  local copies, waits for them, and re-layouts  37 us (21%)
  starting transfers between devices  20.5 us (12%)
  between operations  13.7 us (8%)
  other arithmetic  4.93 us (3%)
    psum x1, waiting for transfers between devices, local(): increment = lax.psum(member_sum, 'mem')  32.7 us
    dot_general x2, matrix products, localize(): jnp.einsum('ij,mljk->mlik', band_lon, extended, preferred_element_type=jn...  24.4 us
    dot_general x2, matrix products, localize(): jnp.einsum('mlibk,kq->mlibq', windows, band_blocks, preferred_element_typ...  23 us
    dot_general x2, local copies, waits for them, and re-layouts, localize(): jnp.einsum('mlibk,kq->mlibq', windows, band_blocks, preferred_element_typ...  12.8 us
    reshape x2, local copies, waits for them, and re-layouts, localize(): return result.reshape(members_here, levels, lon_cells, lat_cells)  9.75 us
    ppermute x3, starting transfers between devices, extended_2(): lax.ppermute(lax.slice_in_dim(block, block.shape[dim] - width, None, axis...  7.17 us
    all_to_all x1, waiting for transfers between devices, local(): lax.all_to_all(weights, 'tile', split_axis=1, concat_axis=0, tiled=True)  5.65 us
    all_to_all x1, starting transfers between devices, local(): lax.all_to_all(cell_index, 'tile', split_axis=1, concat_axis=0, tiled=True)  4.92 us
  transfers between devices with their start and end apart: 10, of which 6 were waited for; matrix products, arithmetic and copies ran while one was open for 30% of the time, Pallas kernels for 0%

commit v1 on v0

--- a/solution.py
+++ b/solution.py
@@ -142,7 +142,8 @@
     col_index = cells_hit % lat_cells
     row_count = levels * lon_cells
     block_rows = math.gcd(observed.shape[0], 1024)
-    increment = lax.psum(member_sum, "mem")
+    parts = lax.all_gather(member_sum, "mem", axis=0, tiled=False)
+    increment = parts.sum(axis=0)
     at_cells = pick_cells(increment.reshape(row_count, lat_cells), row_index, col_index, block_rows)
     misfit = weight_recv * (at_cells - observed)
     spread = spread_cells(misfit, row_index, col_index, row_count, lat_cells, block_rows)

time: 178 us -> 146 us (0.82)
  waiting for transfers between devices: 46.7 us -> 13.8 us
  between operations: 13.7 us -> 0.35 us
  blocking collectives: 0 us -> 13.1 us
    psum x1 -> x0, waiting for transfers between devices: 32.7 us -> none  [local(): increment = lax.psum(member_sum, 'mem')]
    all_gather x0 -> x1, blocking collectives: none -> 13.1 us  [local(): parts = lax.all_gather(member_sum, 'mem', axis=0, tiled=False)]
  transfers between devices with their start and end apart: 10 -> 9, of which waited for: 6 -> 5; matrix products, arithmetic and copies ran while one was open for 30% -> 35% of each run, Pallas kernels for 0% -> 0%
where the time goes in v1:
time: 146 us; the launch traced here: 144 us
  matrix products  53.7 us (37%)
  local copies, waits for them, and re-layouts  36.1 us (25%)
  starting transfers between devices  22.2 us (15%)
  waiting for transfers between devices  13.8 us (9%)
  blocking collectives  13.1 us (9%)
  other arithmetic  4.32 us (3%)
    dot_general x2, matrix products, localize(): jnp.einsum('ij,mljk->mlik', band_lon, extended, preferred_element_type=jn...  24.3 us
    dot_general x2, matrix products, localize(): jnp.einsum('mlibk,kq->mlibq', windows, band_blocks, preferred_element_typ...  22.9 us
    all_gather x1, blocking collectives, local(): parts = lax.all_gather(member_sum, 'mem', axis=0, tiled=False)  13.1 us
    dot_general x2, local copies, waits for them, and re-layouts, localize(): jnp.einsum('mlibk,kq->mlibq', windows, band_blocks, preferred_element_typ...  12.8 us
    reshape x2, local copies, waits for them, and re-layouts, localize(): return result.reshape(members_here, levels, lon_cells, lat_cells)  9.75 us
    ppermute x3, starting transfers between devices, extended_2(): lax.ppermute(lax.slice_in_dim(block, block.shape[dim] - width, None, axis...  8.94 us
    all_to_all x1, waiting for transfers between devices, local(): lax.all_to_all(weights, 'tile', split_axis=1, concat_axis=0, tiled=True)  5.66 us
    all_to_all x1, starting transfers between devices, local(): lax.all_to_all(cell_index, 'tile', split_axis=1, concat_axis=0, tiled=True)  4.92 us
  transfers between devices with their start and end apart: 9, of which 5 were waited for; matrix products, arithmetic and copies ran while one was open for 35% of the time, Pallas kernels for 0%

profile of v1, /device:TPU:11, one launch (start us, length us, event | category | flops | bytes accessed | tf_op | source)
XLA Modules:
  0.0 143.7 jit_solution(11387983166309792231)
XLA Ops:
  0.0 1.5 %fusion.166 = (bf16[20,1,16,720]{3,2,0,1:T(8,128)(2,1)S(1)}, bf16[20,1,16,720]{3,2,0,1:T(8,128)(2,1)S(1)}) fusion(bf16[20,1,45,720]{3,2,0,1:T(8,128)(2,1)} %bitcast.146), kind=kLoop, calls=%fused_computation.199 | loop fusion | bytes 1843200 | tf_op jit(solution)/shard_map/slice | solution.py:15
  1.5 1.8 %collective-permute-start.2 = (bf16[20,1,16,720]{3,2,0,1:T(8,128)(2,1)S(1)}, bf16[20,1,16,720]{3,2,0,1:T(8,128)(2,1)}, u32[]{:S(2)}, u32[]{:S(2)}) collective-permute-start(bf16[20,1,16,720]{3,2,0,1:T(8,128)(2,1)S(1)} %get-tuple-element.110), channel_id=1, source_target_pairs={{0,4},{4,8},{8,12},{12,16},{16,20},{20,24},{24,28},{28,0},{1,5},{5... | collective-permute-start | bytes 1382408 | tf_op jit(solution)/shard_map/ppermute | solution.py:14
  3.4 1.3 copy.62
  4.7 4.9 %all-to-all-start = ((s32[1,8,256]{2,0,1:T(1,128)}), s32[1,8,256]{2,0,1:T(1,128)S(1)}, u32[]{:S(2)}, u32[]{:S(2)}) async-start(s32[1,8,256]{2,0,1:T(1,128)} %copy.62), calls=%async_computation | async-start | bytes 16384 | tf_op jit(solution)/shard_map/all_to_all | solution.py:136
  9.6 2.2 %fusion.167 = (bf16[20,1,16,720]{3,2,0,1:T(8,128)(2,1)}, bf16[20,1,16,720]{3,2,0,1:T(8,128)(2,1)S(1)}) fusion(bf16[20,1,45,720]{3,2,0,1:T(8,128)(2,1)} %bitcast.148), kind=kLoop, calls=%fused_computation.200 | loop fusion | bytes 1843200 | tf_op jit(solution)/shard_map/slice | solution.py:15
  11.8 1.5 %collective-permute-start = (bf16[20,1,16,720]{3,2,0,1:T(8,128)(2,1)}, bf16[20,1,16,720]{3,2,0,1:T(8,128)(2,1)}, u32[]{:S(2)}, u32[]{:S(2)}) collective-permute-start(bf16[20,1,16,720]{3,2,0,1:T(8,128)(2,1)} %get-tuple-element.112), channel_id=1, source_target_pairs={{0,4},{4,8},{8,12},{12,16},{16,20},{20,24},{24,28},{28,0},{1,5},{5... | collective-permute-start | bytes 1382408 | tf_op jit(solution)/shard_map/ppermute | solution.py:14
  13.3 0.7 fusion.170
  14.0 0.7 fusion.169
  14.7 0.7 compare_select_fusion
  15.4 0.6 copy.71
  16.0 0.7 all-to-all-done
  16.7 4.4 %all-to-all-start.1 = ((f32[1,8,256]{2,0,1:T(1,128)}), f32[1,8,256]{2,0,1:T(1,128)S(1)}, u32[]{:S(2)}, u32[]{:S(2)}) async-start(f32[1,8,256]{2,0,1:T(1,128)} %compare_select_fusion), calls=%async_computation.1 | async-start | bytes 16384 | tf_op jit(solution)/shard_map/all_to_all | solution.py:135
  21.1 0.1 remainder_reduce_fusion
  21.2 5.7 %all-to-all-done.1 = f32[1,8,256]{2,0,1:T(1,128)S(1)} async-done(((f32[1,8,256]{2,0,1:T(1,128)}), f32[1,8,256]{2,0,1:T(1,128)S(1)}, u32[]{:S(2)}, u32[]{:S(2)}) %all-to-all-start.1) | async-done | bytes 8224 | tf_op jit(solution)/shard_map/all_to_all | solution.py:135
  26.8 4.0 %all-to-all-start.2 = ((f32[1,8,256]{2,0,1:T(1,128)}), f32[1,8,256]{2,0,1:T(1,128)S(1)}, u32[]{:S(2)}, u32[]{:S(2)}) async-start(f32[1,8,256]{2,0,1:T(1,128)} %copy.71), calls=%async_computation.2 | async-start | bytes 16384 | tf_op jit(solution)/shard_map/all_to_all | solution.py:134
  31.0 3.0 %all-to-all-done.2 = f32[1,8,256]{2,0,1:T(1,128)S(1)} async-done(((f32[1,8,256]{2,0,1:T(1,128)}), f32[1,8,256]{2,0,1:T(1,128)S(1)}, u32[]{:S(2)}, u32[]{:S(2)}) %all-to-all-start.2) | async-done | bytes 8224 | tf_op jit(solution)/shard_map/all_to_all | solution.py:134
  34.0 12.1 %fusion.31 = bf16[20,1,45,720]{3,2,0,1:T(8,128)(2,1)S(1)} fusion(bf16[20,1,16,720]{3,2,0,1:T(8,128)(2,1)} %collective-permute-done.3, bf16[20,1,45,720]{3,2,0,1:T(8,128)(2,1)S(1)} %bitcast.147, bf16[20,1,16,720]{3,2,0,1:T(8,128)(2,1)} %collective-permute-done.2, f32[]{:T(128)} %bitcast.31, f32[]{:T(128)} %bitcast.30, f32[]{:T(128)} %bitcast.29, ...), kind=kOutput, calls=%fused_computation.44 | convolution fusion | flops 107279912 | bytes 3513668 | tf_op jit(solution)/shard_map/ij,mljk->mlik/dot_general | solution.py:46
  46.1 0.2 fusion.33
  46.3 0.2 fusion.44
  46.5 0.2 fusion.43
  46.8 0.2 fusion.35
  47.0 11.4 %fusion.25 = f32[20,45,5,144]{3,1,2,0:T(8,128)S(1)} fusion(f32[]{:T(128)} %bitcast.58, f32[]{:T(128)} %bitcast.57, f32[]{:T(128)} %bitcast.56, f32[]{:T(128)} %bitcast.55, f32[]{:T(128)} %bitcast.54, f32[]{:T(128)} %bitcast.53, f32[]{:T(128)} %bitcast.52, f32[]{:T(128)} %bitcast.51, f32[]{:T(128)} %bitcast.50, f32[]{:T(128)} %bitcast.49, f32[]{:T(128)} %bitcast.48, ...), kind=kOutput, calls=%fused_computation.38 | convolution fusion | flops 229439232 | bytes 4176772 | tf_op jit(solution)/shard_map/mlibk,kq->mlibq/dot_general | solution.py:59
  58.4 6.4 %copy.69 = f32[20,45,5,144]{3,2,1,0:T(8,128)} copy(f32[20,45,5,144]{3,1,2,0:T(8,128)S(1)} %fusion.25) | data formatting | bytes 5184000 | tf_op jit(solution)/shard_map/mlibk,kq->mlibq/dot_general | solution.py:59
  64.8 4.9 %reshape.137 = f32[20,1,45,720]{3,2,0,1:T(8,128)S(1)} reshape(f32[20,45,5,144]{3,2,1,0:T(8,128)} %copy.69) | data formatting | bytes 5184000 | tf_op jit(solution)/shard_map/reshape | solution.py:60
  69.7 1.7 %multiply_reduce_fusion = f32[45,720]{1,0:T(8,128)S(1)} fusion(f32[20,1,45,720]{3,2,0,1:T(8,128)S(1)} %reshape.137, bf16[20,1,45,720]{3,2,1,0:T(8,128)(2,1)} %param.13), kind=kLoop, calls=%fused_computation.22 | loop fusion | flops 1911600 | bytes 4017600 | tf_op jit(solution)/shard_map/reduce_sum | solution.py:129
  71.4 13.1 %all-gather.1 = f32[4,45,720]{2,1,0:T(8,128)S(1)} all-gather(f32[1,45,720]{2,1,0:T(8,128)S(1)} %bitcast.150), channel_id=2, replica_groups=mesh['tile'=8,'mem'=4] {'mem'}, dimensions={0}, use_global_device_ids=true | all-gather | bytes 648000 | tf_op jit(solution)/shard_map/all_gather | solution.py:145
  84.5 0.2 copy.70
  84.7 3.8 %while.21 = (s32[]{:T(128)}, f32[2,1024]{1,0:T(2,128)S(1)}, s32[2,1024]{1,0:T(2,128)S(1)}, s32[2,1024]{1,0:T(2,128)S(1)}, f32[720,45]{1,0:T(8,128)S(1)}, /*index=5*/s32[]{:T(128)}, s32[]{:T(128)}) while((s32[]{:T(128)}, f32[2,1024]{1,0:T(2,128)S(1)}, s32[2,1024]{1,0:T(2,128)S(1)}, s32[2,1024]{1,0:T(2,128)S(1)}, f32[720,45]{1,0:T(8,128)S(1)}, ...), condition=%wide.region_4.5_spmd, body=%wide.region_2.4_spmd.sunk | while | flops 399005696 | bytes 166549 | solution.py:83
  84.7 1.8 %fusion.179 = f32[1024]{0:T(1024)S(1)} fusion(f32[720,45]{1,0:T(8,128)S(1)} %get-tuple-element.240, s32[1024]{0:T(1024)S(1)} %bitcast.158, s32[1024]{0:T(1024)S(1)} %bitcast.159), kind=kOutput, calls=%fused_computation.4.clone.1 | convolution fusion | flops 399005696 | bytes 141888 | tf_op jit(solution)/shard_map/while/body/eval_jaxpr/dot_general | solution.py:75
  86.5 0.1 dynamic_update_slice.5
  86.6 1.8 %fusion.179 = f32[1024]{0:T(1024)S(1)} fusion(f32[720,45]{1,0:T(8,128)S(1)} %get-tuple-element.240, s32[1024]{0:T(1024)S(1)} %bitcast.158, s32[1024]{0:T(1024)S(1)} %bitcast.159), kind=kOutput, calls=%fused_computation.4.clone.1 | convolution fusion | flops 399005696 | bytes 141888 | tf_op jit(solution)/shard_map/while/body/eval_jaxpr/dot_general | solution.py:75
  88.4 0.1 dynamic_update_slice.5
  88.5 3.1 %while.22 = (s32[]{:T(128)}, f32[45,720]{1,0:T(8,128)S(1)}, s32[2,1024]{1,0:T(2,128)S(1)}, f32[2,1024]{1,0:T(2,128)S(1)}, s32[2,1024]{1,0:T(2,128)S(1)}, /*index=5*/s32[]{:T(128)}, s32[]{:T(128)}) while((s32[]{:T(128)}, f32[45,720]{1,0:T(8,128)S(1)}, s32[2,1024]{1,0:T(2,128)S(1)}, f32[2,1024]{1,0:T(2,128)S(1)}, ...), condition=%wide.region_6.7_spmd.clone, body=%wide.region_5.6_spmd.clone.sunk | while | flops 399025440 | bytes 296159 | solution.py:117
  88.6 1.5 %fusion.181 = f32[45,720]{1,0:T(8,128)S(1)} fusion(s32[1024]{0:T(1024)S(1)} %bitcast.156, f32[1024]{0:T(1024)S(1)} %bitcast.154, s32[1024]{0:T(1024)S(1)} %bitcast.157, f32[45,720]{1,0:T(8,128)S(1)} %get-tuple-element.251, pred[]{:T(512)S(6)} %compare.5), kind=kOutput, calls=%fused_computation.11.clone.1 | convolution fusion | flops 399025440 | bytes 271489 | tf_op jit(solution)/shard_map/while/body/eval_jaxpr/dot_general | solution.py:102
  90.2 1.5 %fusion.181 = f32[45,720]{1,0:T(8,128)S(1)} fusion(s32[1024]{0:T(1024)S(1)} %bitcast.156, f32[1024]{0:T(1024)S(1)} %bitcast.154, s32[1024]{0:T(1024)S(1)} %bitcast.157, f32[45,720]{1,0:T(8,128)S(1)} %get-tuple-element.251, pred[]{:T(512)S(6)} %compare.5), kind=kOutput, calls=%fused_computation.11.clone.1 | convolution fusion | flops 399025440 | bytes 271489 | tf_op jit(solution)/shard_map/while/body/eval_jaxpr/dot_general | solution.py:102
  91.7 5.6 %collective-permute-start.4 = (f32[1,16,720]{2,1,0:T(8,128)S(1)}, f32[1,16,720]{2,1,0:T(8,128)S(1)}, u32[]{:S(2)}, u32[]{:S(2)}) collective-permute-start(f32[1,16,720]{2,1,0:T(8,128)S(1)} %get-tuple-element.114), channel_id=1, source_target_pairs={{0,4},{4,8},{8,12},{12,16},{16,20},{20,24},{24,28},{28,0},{1,5},{5... | collective-permute-start | bytes 138248 | tf_op jit(solution)/shard_map/ppermute | solution.py:14
  97.3 1.2 collective-permute-done.4
  98.5 3.2 %collective-permute-done.5 = f32[1,16,720]{2,1,0:T(8,128)S(1)} collective-permute-done((f32[1,16,720]{2,1,0:T(8,128)S(1)}, f32[1,16,720]{2,1,0:T(8,128)S(1)}, u32[]{:S(2)}, u32[]{:S(2)}) %collective-permute-start.5) | collective-permute-done | bytes 46112 | tf_op jit(solution)/shard_map/ppermute | solution.py:17
  101.8 12.3 %fusion.30 = bf16[20,1,45,720]{3,2,0,1:T(8,128)(2,1)S(1)} fusion(bf16[20,16,720]{2,1,0:T(8,128)(2,1)} %bitcast.8, bf16[20,45,720]{2,1,0:T(8,128)(2,1)S(1)} %bitcast.149, bf16[20,16,720]{2,1,0:T(8,128)(2,1)} %bitcast.5, f32[77,720]{1,0:T(8,128)S(1)} %maximum_bitcast_fusion.6, f32[]{:T(128)} %bitcast.31, f32[]{:T(128)} %bitcast.30, f32[]{:T(128)} %bitcast.29, ...), kind=kOutput, calls=%fused_computation.43 | convolution fusion | flops 109497512 | bytes 3735428 | tf_op jit(solution)/shard_map/ij,mljk->mlik/dot_general | solution.py:46
  114.1 0.2 fusion.37
  114.3 0.2 fusion.41
  114.5 0.2 fusion.40
  114.7 0.2 fusion.39
  115.0 11.4 %fusion.23 = f32[20,45,5,144]{3,1,2,0:T(8,128)S(1)} fusion(f32[]{:T(128)} %bitcast.58, f32[]{:T(128)} %bitcast.57, f32[]{:T(128)} %bitcast.56, f32[]{:T(128)} %bitcast.55, f32[]{:T(128)} %bitcast.54, f32[]{:T(128)} %bitcast.53, f32[]{:T(128)} %bitcast.52, f32[]{:T(128)} %bitcast.51, f32[]{:T(128)} %bitcast.50, f32[]{:T(128)} %bitcast.49, f32[]{:T(128)} %bitcast.48, ...), kind=kOutput, calls=%fused_computation.36 | convolution fusion | flops 229439232 | bytes 4176772 | tf_op jit(solution)/shard_map/mlibk,kq->mlibq/dot_general | solution.py:59
  126.4 6.4 %copy.73 = f32[20,45,5,144]{3,2,1,0:T(8,128)} copy(f32[20,45,5,144]{3,1,2,0:T(8,128)S(1)} %fusion.23) | data formatting | bytes 5184000 | tf_op jit(solution)/shard_map/mlibk,kq->mlibq/dot_general | solution.py:59
  132.8 4.9 %reshape.141 = f32[20,1,45,720]{3,2,0,1:T(8,128)S(1)} reshape(f32[20,45,5,144]{3,2,1,0:T(8,128)} %copy.73) | data formatting | bytes 5184000 | tf_op jit(solution)/shard_map/reshape | solution.py:60
  137.7 1.7 %convert_add_fusion = f32[20,1,45,720]{3,2,0,1:T(8,128)S(1)} fusion(f32[20,1,45,720]{3,2,0,1:T(8,128)S(1)} %reshape.141, bf16[20,1,45,720]{3,2,1,0:T(8,128)(2,1)} %param.12), kind=kLoop, calls=%fused_computation.23 | loop fusion | flops 1296000 | bytes 6480000 | tf_op jit(solution)/shard_map/add | solution.py:154
  139.3 4.4 %copy.74 = f32[20,1,45,720]{3,1,2,0:T(1,128)} copy(f32[20,1,45,720]{3,2,0,1:T(8,128)S(1)} %convert_add_fusion) | data formatting | bytes 5184000 | tf_op jit(solution)/shard_map/add | solution.py:154
  (47 shorter events, 0.4 us)
Async XLA Ops:
  0.0 34.0 %copy-start = (bf16[20,1,45,720]{3,2,1,0:T(8,128)(2,1)S(1)}, bf16[20,1,45,720]{3,2,1,0:T(8,128)(2,1)}, u32[]{:S(2)}) copy-start(bf16[20,1,45,720]{3,2,1,0:T(8,128)(2,1)} %param.12) | copy-start | bytes 3888004
  0.0 13.2 %copy-start.3 = (bf16[17]{0:T(256)(128)(2,1)S(1)}, bf16[17]{0:T(256)(128)(2,1)}, u32[]{:S(2)}) copy-start(bf16[17]{0:T(256)(128)(2,1)} %param.14) | copy-start | bytes 106
  0.0 14.0 %copy-start.4 = (bf16[17]{0:T(256)(128)(2,1)S(1)}, bf16[17]{0:T(256)(128)(2,1)}, u32[]{:S(2)}) copy-start(bf16[17]{0:T(256)(128)(2,1)} %param.15) | copy-start | bytes 106
  0.0 14.7 %copy-start.7 = (s32[1,8]{1,0:T(1,128)S(1)}, s32[1,8]{1,0:T(1,128)}, u32[]{:S(2)}) copy-start(s32[1,8]{1,0:T(1,128)} %param.19) | copy-start | bytes 100
  0.0 14.7 %copy-start.5 = (f32[1,8,256]{2,1,0:T(8,128)S(1)}, f32[1,8,256]{2,1,0:T(8,128)}, u32[]{:S(2)}) copy-start(f32[1,8,256]{2,1,0:T(8,128)} %param.17) | copy-start | bytes 24580
  0.0 15.4 %copy-start.6 = (f32[1,8,256]{2,1,0:T(8,128)S(1)}, f32[1,8,256]{2,1,0:T(8,128)}, u32[]{:S(2)}) copy-start(f32[1,8,256]{2,1,0:T(8,128)} %param.16) | copy-start | bytes 24580
  1.5 32.4 %collective-permute-start.2 = (bf16[20,1,16,720]{3,2,0,1:T(8,128)(2,1)S(1)}, bf16[20,1,16,720]{3,2,0,1:T(8,128)(2,1)}, u32[]{:S(2)}, u32[]{:S(2)}) collective-permute-start(bf16[20,1,16,720]{3,2,0,1:T(8,128)(2,1)S(1)} %get-tuple-element.110), channel_id=1, source_target_pairs={{0,4},{4,8},{8,12},{12,16},{16,20},{20,24},{24,28},{28,0},{1,5},{5... | collective-permute-start | bytes 1382408 | tf_op jit(solution)/shard_map/ppermute | solution.py:14
  3.4 30.6 %collective-permute-start.3 = (bf16[20,1,16,720]{3,2,0,1:T(8,128)(2,1)S(1)}, bf16[20,1,16,720]{3,2,0,1:T(8,128)(2,1)}, u32[]{:S(2)}, u32[]{:S(2)}) collective-permute-start(bf16[20,1,16,720]{3,2,0,1:T(8,128)(2,1)S(1)} %get-tuple-element.111), channel_id=1, source_target_pairs={{4,0},{8,4},{12,8},{16,12},{20,16},{24,20},{28,24},{0,28},{5,1},{9... | collective-permute-start | bytes 1382408 | tf_op jit(solution)/shard_map/ppermute | solution.py:17
  4.7 12.0 %all-to-all-start = ((s32[1,8,256]{2,0,1:T(1,128)}), s32[1,8,256]{2,0,1:T(1,128)S(1)}, u32[]{:S(2)}, u32[]{:S(2)}) async-start(s32[1,8,256]{2,0,1:T(1,128)} %copy.62), calls=%async_computation | async-start | bytes 16384 | tf_op jit(solution)/shard_map/all_to_all | solution.py:136
  11.8 90.0 %collective-permute-start = (bf16[20,1,16,720]{3,2,0,1:T(8,128)(2,1)}, bf16[20,1,16,720]{3,2,0,1:T(8,128)(2,1)}, u32[]{:S(2)}, u32[]{:S(2)}) collective-permute-start(bf16[20,1,16,720]{3,2,0,1:T(8,128)(2,1)} %get-tuple-element.112), channel_id=1, source_target_pairs={{0,4},{4,8},{8,12},{12,16},{16,20},{20,24},{24,28},{28,0},{1,5},{5... | collective-permute-start | bytes 1382408 | tf_op jit(solution)/shard_map/ppermute | solution.py:14
  13.2 88.5 %collective-permute-start.1 = (bf16[20,1,16,720]{3,2,0,1:T(8,128)(2,1)S(1)}, bf16[20,1,16,720]{3,2,0,1:T(8,128)(2,1)}, u32[]{:S(2)}, u32[]{:S(2)}) collective-permute-start(bf16[20,1,16,720]{3,2,0,1:T(8,128)(2,1)S(1)} %get-tuple-element.113), channel_id=1, source_target_pairs={{4,0},{8,4},{12,8},{16,12},{20,16},{24,20},{28,24},{0,28},{5,1},{9... | collective-permute-start | bytes 1382408 | tf_op jit(solution)/shard_map/ppermute | solution.py:17
  16.7 10.1 %all-to-all-start.1 = ((f32[1,8,256]{2,0,1:T(1,128)}), f32[1,8,256]{2,0,1:T(1,128)S(1)}, u32[]{:S(2)}, u32[]{:S(2)}) async-start(f32[1,8,256]{2,0,1:T(1,128)} %compare_select_fusion), calls=%async_computation.1 | async-start | bytes 16384 | tf_op jit(solution)/shard_map/all_to_all | solution.py:135
  26.8 7.1 %all-to-all-start.2 = ((f32[1,8,256]{2,0,1:T(1,128)}), f32[1,8,256]{2,0,1:T(1,128)S(1)}, u32[]{:S(2)}, u32[]{:S(2)}) async-start(f32[1,8,256]{2,0,1:T(1,128)} %copy.71), calls=%async_computation.2 | async-start | bytes 16384 | tf_op jit(solution)/shard_map/all_to_all | solution.py:134
  84.7 3.8 %copy-start.2 = (f32[45,720]{1,0:T(8,128)S(1)}, f32[45,720]{1,0:T(8,128)}, u32[]{:S(2)}) copy-start(f32[45,720]{1,0:T(8,128)} %custom-call) | copy-start | bytes 388804
  88.5 13.3 %copy-start.1 = (bf16[20,1,45,720]{3,2,1,0:T(8,128)(2,1)S(1)}, bf16[20,1,45,720]{3,2,1,0:T(8,128)(2,1)}, u32[]{:S(2)}) copy-start(bf16[20,1,45,720]{3,2,1,0:T(8,128)(2,1)} %param.13) | copy-start | bytes 3888004
  91.7 6.8 %collective-permute-start.4 = (f32[1,16,720]{2,1,0:T(8,128)S(1)}, f32[1,16,720]{2,1,0:T(8,128)S(1)}, u32[]{:S(2)}, u32[]{:S(2)}) collective-permute-start(f32[1,16,720]{2,1,0:T(8,128)S(1)} %get-tuple-element.114), channel_id=1, source_target_pairs={{0,4},{4,8},{8,12},{12,16},{16,20},{20,24},{24,28},{28,0},{1,5},{5... | collective-permute-start | bytes 138248 | tf_op jit(solution)/shard_map/ppermute | solution.py:14
  97.3 4.4 %collective-permute-start.5 = (f32[1,16,720]{2,1,0:T(8,128)S(1)}, f32[1,16,720]{2,1,0:T(8,128)S(1)}, u32[]{:S(2)}, u32[]{:S(2)}) collective-permute-start(f32[1,16,720]{2,1,0:T(8,128)S(1)} %get-tuple-element.115), channel_id=1, source_target_pairs={{4,0},{8,4},{12,8},{16,12},{20,16},{24,20},{28,24},{0,28},{5,1},{9... | collective-permute-start | bytes 138248 | tf_op jit(solution)/shard_map/ppermute | solution.py:17
